TPU v7x, 32 devices: a whole 2x2x4 slice. The times are simulated.
32 devices in a mesh: dp: 4 (over y, x), seq: 8 (over z, core).
Axes of the slice: x: 2, y: 2, z: 4, core: 2. Of those that a mesh axis runs over, the one named last changes fastest.
Arguments:
- queries: bfloat16 [6144, 2048], P(('dp', 'seq')), may hold values from -16 to 16
- keys: bfloat16 [6144, 2048], P(('dp', 'seq')), may hold values from -16 to 16
- values: bfloat16 [6144, 2048], P(('dp', 'seq')), may hold values from -6 to 6
- out_grad: bfloat16 [6144, 2048], P(('dp', 'seq')), may hold values from -6 to 6
- out_weight: bfloat16 [2048, 2048], P('dp'), may hold values from -0.125 to 0.125
- section_ids: int32 [6144], P(('dp', 'seq')), may hold values from 0 to 95, as said below
- masked: int32 [6144], P(('dp', 'seq')), may hold values from 0 to 1, as said below
Outputs:
- query_grad: bfloat16 [6144, 2048], P(('dp', 'seq'))
- key_grad: bfloat16 [6144, 2048], P(('dp', 'seq'))
- value_grad: bfloat16 [6144, 2048], P(('dp', 'seq'))
- weight_grad: float32 [2048, 2048], P('dp')
Inputs may be any that keep to these rules, and one draw needn't show every extreme that they name: `section_ids`: section numbers never fall along the tokens, are constant over each aligned block of 64 tokens, and no section spans two sequences of 1536 tokens. `masked`: the same for all tokens of a section.
All inputs are finite; a program needn't handle non-finite values.
Results may differ from a plain program's by a relative error of at most 0.015.
Values may be sent and summed in bfloat16 or wider, within the bound.
No kernel may reach another device: no remote copies, remote signals or barrier semaphores. Data moves between devices by JAX's collectives and lax.ppermute only.
A program may use at most 128 MiB of HBM per device.

v0:
```python
import jax
import jax.numpy as jnp
from jax import lax
from jax.sharding import PartitionSpec as P

HEAD_DIM = 128


def local(queries, keys, values, out_grad, out_weight, section_ids, masked):
    score_scale = HEAD_DIM ** (-0.5)
    attn_grad = lax.dot_general(
        out_grad,
        lax.all_gather(out_weight, "dp", axis=0, tiled=True),
        (((1,), (1,)), ((), ())),
        preferred_element_type=jnp.float32,
    ).astype(jnp.bfloat16)
    query_h, key_h, value_h = (
        lax.all_to_all(queries, "seq", split_axis=1, concat_axis=0, tiled=True),
        lax.all_to_all(keys, "seq", split_axis=1, concat_axis=0, tiled=True),
        lax.all_to_all(values, "seq", split_axis=1, concat_axis=0, tiled=True),
    )
    grad_h = lax.all_to_all(attn_grad, "seq", split_axis=1, concat_axis=0, tiled=True)
    sec_all, flag_all = (
        lax.all_gather(section_ids, "seq", axis=0, tiled=True),
        lax.all_gather(masked, "seq", axis=0, tiled=True),
    )
    seq_span = query_h.shape[0]
    width_here = query_h.shape[1]
    heads_here = width_here // HEAD_DIM
    block_rows = min(512, seq_span)
    num_blocks = seq_span // block_rows
    keys_head = key_h.reshape(seq_span, heads_here, HEAD_DIM)
    values_head = value_h.reshape(seq_span, heads_here, HEAD_DIM)
    visible_key = flag_all == 0

    def block_step(carried, block_item):
        key_acc, value_acc = carried
        query_blk, grad_blk, sec_blk = block_item
        scores = (
            jnp.einsum("qhd,khd->hqk", query_blk, keys_head, preferred_element_type=jnp.float32)
            * score_scale
        )
        allowed = visible_key[None, :] | (sec_blk[:, None] == sec_all[None, :])
        scores = jnp.where(allowed[None], scores, -1e30)
        row_max = jnp.max(scores, axis=2, keepdims=True)
        exp_scores = jnp.exp(scores - row_max)
        attn_probs = exp_scores / jnp.sum(exp_scores, axis=2, keepdims=True)
        probs_low = attn_probs.astype(jnp.bfloat16)
        out_blk = jnp.einsum(
            "hqk,khd->qhd", probs_low, values_head, preferred_element_type=jnp.float32
        ).astype(jnp.bfloat16)
        row_delta = jnp.sum(grad_blk.astype(jnp.float32) * out_blk.astype(jnp.float32), axis=2)
        prob_grad = jnp.einsum(
            "qhd,khd->hqk", grad_blk, values_head, preferred_element_type=jnp.float32
        )
        score_grad = (attn_probs * (prob_grad - row_delta.T[:, :, None])).astype(jnp.bfloat16)
        query_blk_grad = (
            jnp.einsum("hqk,khd->qhd", score_grad, keys_head, preferred_element_type=jnp.float32)
            * score_scale
        ).astype(jnp.bfloat16)
        key_acc = key_acc + jnp.einsum(
            "hqk,qhd->khd", score_grad, query_blk, preferred_element_type=jnp.float32
        )
        value_acc = value_acc + jnp.einsum(
            "hqk,qhd->khd", probs_low, grad_blk, preferred_element_type=jnp.float32
        )
        return ((key_acc, value_acc), (out_blk, query_blk_grad))

    scan_inputs = (
        query_h.reshape(num_blocks, block_rows, heads_here, HEAD_DIM),
        grad_h.reshape(num_blocks, block_rows, heads_here, HEAD_DIM),
        sec_all.reshape(num_blocks, block_rows),
    )
    zero_acc = jnp.zeros((seq_span, heads_here, HEAD_DIM), jnp.float32)
    (key_acc, value_acc), (out_blocks, query_blocks) = lax.scan(
        block_step, (zero_acc, zero_acc), scan_inputs
    )
    out_head = out_blocks.reshape(seq_span, width_here)
    query_grad_h = query_blocks.reshape(seq_span, width_here)
    key_grad_h = (key_acc * score_scale).astype(jnp.bfloat16).reshape(seq_span, width_here)
    value_grad_h = value_acc.astype(jnp.bfloat16).reshape(seq_span, width_here)
    attn_out, query_grad, key_grad, value_grad = (
        lax.all_to_all(out_head, "seq", split_axis=0, concat_axis=1, tiled=True),
        lax.all_to_all(query_grad_h, "seq", split_axis=0, concat_axis=1, tiled=True),
        lax.all_to_all(key_grad_h, "seq", split_axis=0, concat_axis=1, tiled=True),
        lax.all_to_all(value_grad_h, "seq", split_axis=0, concat_axis=1, tiled=True),
    )
    grad_share = lax.psum_scatter(
        lax.dot_general(
            attn_out, out_grad, (((0,), (0,)), ((), ())), preferred_element_type=jnp.float32
        ),
        ("dp", "seq"),
        scatter_dimension=0,
        tiled=True,
    )
    weight_grad = lax.all_gather(grad_share, "seq", axis=0, tiled=True)
    return (query_grad, key_grad, value_grad, weight_grad)


def solution(mesh):
    placed = (
        P(("dp", "seq"), None),
        P(("dp", "seq"), None),
        P(("dp", "seq"), None),
        P(("dp", "seq"), None),
        P("dp", None),
        P(("dp", "seq")),
        P(("dp", "seq")),
    )
    return jax.shard_map(
        local,
        mesh=mesh,
        in_specs=placed,
        out_specs=(
            P(("dp", "seq"), None),
            P(("dp", "seq"), None),
            P(("dp", "seq"), None),
            P("dp", None),
        ),
        check_vma=False,
    )
```

profile of v0, /device:TPU:0, one launch (start us, length us, event | category | flops | bytes accessed | tf_op | source)
XLA Modules:
  0.0 559.5 jit_solution(2714547254245114422)
XLA Ops:
  7.9 2.1 copy.96
  10.1 6.4 %all-to-all-start = ((bf16[192,8,256]{2,0,1:T(8,128)(2,1)}), bf16[192,8,256]{2,0,1:T(8,128)(2,1)S(1)}, u32[]{:S(2)}, u32[]{:S(2)}) async-start(bf16[192,8,256]{2,0,1:T(8,128)(2,1)} %bitcast.78), calls=%async_computation | async-start | bytes 1572864 | tf_op jit(solution)/shard_map/all_to_all | solution.py:18
  17.4 20.0 %all-to-all-done = bf16[192,8,256]{2,0,1:T(8,128)(2,1)S(1)} async-done(((bf16[192,8,256]{2,0,1:T(8,128)(2,1)}), bf16[192,8,256]{2,0,1:T(8,128)(2,1)S(1)}, u32[]{:S(2)}, u32[]{:S(2)}) %all-to-all-start) | async-done | bytes 786464 | tf_op jit(solution)/shard_map/all_to_all | solution.py:18
  37.4 3.5 all-to-all-start.1
  41.9 19.9 %all-to-all-done.1 = bf16[192,8,256]{2,0,1:T(8,128)(2,1)S(1)} async-done(((bf16[192,8,256]{2,0,1:T(8,128)(2,1)}), bf16[192,8,256]{2,0,1:T(8,128)(2,1)S(1)}, u32[]{:S(2)}, u32[]{:S(2)}) %all-to-all-start.1) | async-done | bytes 786464 | tf_op jit(solution)/shard_map/all_to_all | solution.py:19
  61.8 3.5 all-to-all-start.3
  65.4 34.7 %all-gather.3.cloned.1.call-done = bf16[2048,2048]{1,0:T(8,128)(2,1)} async-done(((bf16[512,2048]{1,0:T(8,128)(2,1)}), bf16[2048,2048]{1,0:T(8,128)(2,1)}) %all-gather.3.cloned.1.call-update) | async-done | bytes 8388624 | tf_op jit(solution)/shard_map/all_gather | solution.py:13
  100.1 6.3 %convolution_convert_fusion.1 = bf16[192,2048]{1,0:T(8,128)(2,1)S(1)} fusion(bf16[192,2048]{1,0:T(8,128)(2,1)S(1)} %copy-done, bf16[2048,2048]{1,0:T(8,128)(2,1)} %all-gather.3.cloned.1.call-done), kind=kOutput, calls=%fused_computation.31 | convolution fusion | flops 1611005952 | bytes 9961472 | tf_op jit(solution)/shard_map/dot_general | solution.py:11
  107.4 4.6 all-to-all-start.2
  114.0 35.4 %all-reduce.2 = (s32[1536]{0:T(1024)S(1)}, s32[1536]{0:T(1024)S(1)}) all-reduce(s32[1536]{0:T(1024)S(1)} %dynamic-update-slice, s32[1536]{0:T(1024)S(1)} %dynamic-update-slice.1), channel_id=1, replica_groups=mesh['dp'=4,'seq'=8] {'seq'}, use_global_device_ids=true, to_apply=%add | all-reduce | flops 3072 | bytes 24576
  150.4 2.7 reshape.110
  154.4 2.7 reshape.112
  157.1 3.1 copy.46
  160.2 2.7 reshape.111
  162.9 64.5 %while.17 = (s32[]{:T(128)}, f32[1536,2,128]{0,2,1:T(8,128)}, f32[1536,2,128]{0,2,1:T(8,128)S(1)}, bf16[3,512,2,128]{3,2,1,0:T(2,128)(2,1)}, bf16[3,512,2,128]{3...) while((s32[]{:T(128)}, f32[1536,2,128]{0,2,1:T(8,128)}, ...), condition=%wide.region_4.5_spmd.clone, body=%wide.region_0.4_spmd.clone.sunk | while | flops 2435711488 | bytes 88377160 | solution.py:75
  162.9 1.9 constant_dynamic-slice_fusion.6
  165.9 1.5 compare_or_fusion.2
  167.4 6.1 %fusion.50 = (f32[2,512]{1,0:T(2,128)S(1)}, f32[2,512,1536]{2,1,0:T(8,128)}) fusion(pred[512,1536]{1,0:T(8,128)(4,1)} %compare_or_fusion.2, bf16[1536,2,128]{2,0,1:T(8,128)(2,1)S(1)} %get-tuple-element.290, bf16[1,512,2,128]{3,2,1,0:T(2,128)(2,1)S(1)} %constant_dynamic-slice_fusion.8), kind=kOutput, calls=%fused_computation.38.clone.1 | convolution fusion | flops 408946176 | bytes 8130560 | tf_op jit(solution)/shard_map/while/body/eval_jaxpr/sub | solution.py:46
  173.5 3.8 fusion.51
  183.1 1.3 copy_dynamic-update-slice_fusion.3
  184.4 1.9 constant_dynamic-slice_fusion.6
  187.4 1.5 compare_or_fusion.2
  188.9 6.1 %fusion.50 = (f32[2,512]{1,0:T(2,128)S(1)}, f32[2,512,1536]{2,1,0:T(8,128)}) fusion(pred[512,1536]{1,0:T(8,128)(4,1)} %compare_or_fusion.2, bf16[1536,2,128]{2,0,1:T(8,128)(2,1)S(1)} %get-tuple-element.290, bf16[1,512,2,128]{3,2,1,0:T(2,128)(2,1)S(1)} %constant_dynamic-slice_fusion.8), kind=kOutput, calls=%fused_computation.38.clone.1 | convolution fusion | flops 408946176 | bytes 8130560 | tf_op jit(solution)/shard_map/while/body/eval_jaxpr/sub | solution.py:46
  195.1 3.8 fusion.51
  204.6 1.3 copy_dynamic-update-slice_fusion.3
  205.9 1.9 constant_dynamic-slice_fusion.6
  208.9 1.5 compare_or_fusion.2
  210.4 6.1 %fusion.50 = (f32[2,512]{1,0:T(2,128)S(1)}, f32[2,512,1536]{2,1,0:T(8,128)}) fusion(pred[512,1536]{1,0:T(8,128)(4,1)} %compare_or_fusion.2, bf16[1536,2,128]{2,0,1:T(8,128)(2,1)S(1)} %get-tuple-element.290, bf16[1,512,2,128]{3,2,1,0:T(2,128)(2,1)S(1)} %constant_dynamic-slice_fusion.8), kind=kOutput, calls=%fused_computation.38.clone.1 | convolution fusion | flops 408946176 | bytes 8130560 | tf_op jit(solution)/shard_map/while/body/eval_jaxpr/sub | solution.py:46
  216.6 3.8 fusion.51
  226.1 1.3 copy_dynamic-update-slice_fusion.3
  227.4 2.4 all_to_all.128
  229.9 23.4 %all_to_all.140 = bf16[8,192,256]{2,1,0:T(8,128)(2,1)S(1)} all-to-all(bf16[8,192,256]{2,1,0:T(8,128)(2,1)S(1)} %all_to_all.128), channel_id=1, replica_groups=mesh['dp'=4,'seq'=8] {'seq'}, dimensions={0} | all-to-all | bytes 1572864 | tf_op jit(solution)/shard_map/all_to_all | solution.py:83
  253.3 8.1 %fusion.16 = f32[2048,2048]{1,0:T(8,128)} fusion(bf16[192,2048]{1,0:T(8,128)(2,1)S(1)} %bitcast.122, bf16[192,2048]{1,0:T(8,128)(2,1)S(1)} %copy-done), kind=kOutput, calls=%fused_computation.39 | convolution fusion | flops 1610612736 | bytes 18350080 | tf_op jit(solution)/shard_map/dot_general | solution.py:89
  261.5 184.6 %reduce-scatter.2.cloned.1.call-done = f32[64,2048]{1,0:T(8,128)} async-done(((f32[2048,2048]{1,0:T(8,128)}), f32[64,2048]{1,0:T(8,128)}) %reduce-scatter.2.cloned.1.call-update) | async-done | bytes 524304 | tf_op jit(solution)/shard_map/reduce_scatter | solution.py:88
  446.2 1.4 all_to_all.116
  447.6 3.5 all-to-all-start.4
  451.1 2.5 multiply_convert_fusion.1
  453.6 3.1 copy.49
  456.7 3.1 all_to_all.120
  459.8 31.4 %all-to-all-done.4 = bf16[8,192,256]{2,1,0:T(8,128)(2,1)S(1)} async-done(((bf16[8,192,256]{2,1,0:T(8,128)(2,1)}), bf16[8,192,256]{2,1,0:T(8,128)(2,1)S(1)}, u32[]{:S(2)}, u32[]{:S(2)}) %all-to-all-start.4) | async-done | bytes 786464 | tf_op jit(solution)/shard_map/all_to_all | solution.py:84
  491.2 4.5 all-to-all-start.5
  496.7 2.3 copy.51
  499.0 1.4 all_to_all.124
  500.4 22.5 %all-to-all-done.5 = bf16[8,192,256]{2,1,0:T(8,128)(2,1)} async-done(((bf16[8,192,256]{2,1,0:T(8,128)(2,1)}), bf16[8,192,256]{2,1,0:T(8,128)(2,1)}, u32[]{:S(2)}, u32[]{:S(2)}) %all-to-all-start.5) | async-done | bytes 786464 | tf_op jit(solution)/shard_map/all_to_all | solution.py:85
  522.8 3.5 all-to-all-start.6
  527.4 2.1 copy.70
  529.5 17.8 %all-to-all-done.6 = bf16[8,192,256]{2,1,0:T(8,128)(2,1)S(1)} async-done(((bf16[8,192,256]{2,1,0:T(8,128)(2,1)}), bf16[8,192,256]{2,1,0:T(8,128)(2,1)S(1)}, u32[]{:S(2)}, u32[]{:S(2)}) %all-to-all-start.6) | async-done | bytes 786464 | tf_op jit(solution)/shard_map/all_to_all | solution.py:86
  548.2 4.7 copy.131
  (107 shorter events, 30.6 us)
Async XLA Ops:
  7.2 92.9 %copy-start = (bf16[192,2048]{1,0:T(8,128)(2,1)S(1)}, bf16[192,2048]{1,0:T(8,128)(2,1)}, u32[]{:S(2)}) copy-start(bf16[192,2048]{1,0:T(8,128)(2,1)} %param.12) | copy-start | bytes 2359300
  7.2 9.2 %copy-start.6 = (bf16[192,2048]{1,0:T(8,128)(2,1)S(1)}, bf16[192,2048]{1,0:T(8,128)(2,1)}, u32[]{:S(2)}) copy-start(bf16[192,2048]{1,0:T(8,128)(2,1)} %param.10) | copy-start | bytes 2359300
  7.2 92.9 %all-gather.3.cloned.1.call-start = ((), (), s32[]{:S(2)}) async-start(), calls=%async_computation.9 | async-start | bytes 10485760 | tf_op jit(solution)/shard_map/all_gather | solution.py:13
  7.9 33.0 %copy-start.7 = (bf16[192,2048]{1,0:T(8,128)(2,1)S(1)}, bf16[192,2048]{1,0:T(8,128)(2,1)}, u32[]{:S(2)}) copy-start(bf16[192,2048]{1,0:T(8,128)(2,1)} %param.11) | copy-start | bytes 2359300
  10.1 27.3 %all-to-all-start = ((bf16[192,8,256]{2,0,1:T(8,128)(2,1)}), bf16[192,8,256]{2,0,1:T(8,128)(2,1)S(1)}, u32[]{:S(2)}, u32[]{:S(2)}) async-start(bf16[192,8,256]{2,0,1:T(8,128)(2,1)} %bitcast.78), calls=%async_computation | async-start | bytes 1572864 | tf_op jit(solution)/shard_map/all_to_all | solution.py:18
  37.4 24.4 %all-to-all-start.1 = ((bf16[192,8,256]{2,0,1:T(8,128)(2,1)}), bf16[192,8,256]{2,0,1:T(8,128)(2,1)S(1)}, u32[]{:S(2)}, u32[]{:S(2)}) async-start(bf16[192,8,256]{2,0,1:T(8,128)(2,1)} %bitcast.77), calls=%async_computation.1 | async-start | bytes 1572864 | tf_op jit(solution)/shard_map/all_to_all | solution.py:19
  61.8 44.6 %copy-start.4 = (bf16[192,8,256]{2,0,1:T(8,128)(2,1)}, bf16[192,8,256]{2,0,1:T(8,128)(2,1)S(1)}, u32[]{:S(2)}) copy-start(bf16[192,8,256]{2,0,1:T(8,128)(2,1)S(1)} %all-to-all-done.1) | copy-start | bytes 2359300
  61.8 45.6 %all-to-all-start.3 = ((bf16[192,8,256]{2,0,1:T(8,128)(2,1)}), bf16[192,8,256]{2,0,1:T(8,128)(2,1)S(1)}, u32[]{:S(2)}, u32[]{:S(2)}) async-start(bf16[192,8,256]{2,0,1:T(8,128)(2,1)} %bitcast.127), calls=%async_computation.3 | async-start | bytes 1572864 | tf_op jit(solution)/shard_map/all_to_all | solution.py:20
  106.4 5.8 %copy-start.12 = (u32[32]{0:T(128)S(1)}, u32[32]{0:T(128)}, u32[]{:S(2)}) copy-start(u32[32]{0:T(128)} %constant.33) | copy-start | bytes 388
  106.4 7.0 %copy-start.10 = (s32[192]{0:T(256)S(1)}, s32[192]{0:T(256)}, u32[]{:S(2)}) copy-start(s32[192]{0:T(256)} %param.15) | copy-start | bytes 2308
  106.4 7.3 %copy-start.11 = (s32[192]{0:T(256)S(1)}, s32[192]{0:T(256)}, u32[]{:S(2)}) copy-start(s32[192]{0:T(256)} %param.14) | copy-start | bytes 2308
  107.4 4.7 copy-start.5
  107.4 52.8 %all-to-all-start.2 = ((bf16[192,8,256]{2,0,1:T(8,128)(2,1)}), bf16[192,8,256]{2,0,1:T(8,128)(2,1)}, u32[]{:S(2)}, u32[]{:S(2)}) async-start(bf16[192,8,256]{2,0,1:T(8,128)(2,1)} %bitcast.76), calls=%async_computation.2 | async-start | bytes 1572864 | tf_op jit(solution)/shard_map/all_to_all | solution.py:22
  112.0 334.1 %reduce-scatter.2.cloned.1.call-start = ((), (), s32[]{:S(2)}) async-start(), calls=%async_computation.10 | async-start | bytes 17301504 | tf_op jit(solution)/shard_map/reduce_scatter | solution.py:88
  173.5 3.8 copy-start.3
  173.5 3.8 copy-start.8
  173.5 5.9 %slice-start = ((s8[6291456]{0:T(1024)(128)(4,1)}), s8[4194304]{0:T(1024)(128)(4,1)S(1)}, s32[]{:S(2)}) async-start(s8[6291456]{0:T(1024)(128)(4,1)} %bitcast.119), calls=%async_computation.12 | async-start | bytes 8388608 | tf_op jit(solution)/shard_map/while
  177.3 2.1 slice-start.1
  180.7 1.4 copy-start.1
  183.1 1.4 copy-start.2
  195.1 3.8 copy-start.3
  195.1 3.8 copy-start.8
  195.1 5.9 %slice-start = ((s8[6291456]{0:T(1024)(128)(4,1)}), s8[4194304]{0:T(1024)(128)(4,1)S(1)}, s32[]{:S(2)}) async-start(s8[6291456]{0:T(1024)(128)(4,1)} %bitcast.119), calls=%async_computation.12 | async-start | bytes 8388608 | tf_op jit(solution)/shard_map/while
  198.8 2.1 slice-start.1
  202.2 1.4 copy-start.1
  204.6 1.3 copy-start.2
  216.6 3.8 copy-start.3
  216.6 3.8 copy-start.8
  216.6 5.9 %slice-start = ((s8[6291456]{0:T(1024)(128)(4,1)}), s8[4194304]{0:T(1024)(128)(4,1)S(1)}, s32[]{:S(2)}) async-start(s8[6291456]{0:T(1024)(128)(4,1)} %bitcast.119), calls=%async_computation.12 | async-start | bytes 8388608 | tf_op jit(solution)/shard_map/while
  220.4 2.1 slice-start.1
  223.7 1.4 copy-start.1
  226.1 1.3 copy-start.2
  261.4 184.7 %copy-start.9 = (bf16[3,512,2,128]{3,2,1,0:T(2,128)(2,1)S(1)}, bf16[3,512,2,128]{3,2,1,0:T(2,128)(2,1)}, u32[]{:S(2)}) copy-start(bf16[3,512,2,128]{3,2,1,0:T(2,128)(2,1)} %get-tuple-element.69) | copy-start | bytes 2359300
  261.5 286.8 %all-gather.5.cloned.1.call-start = ((), (), s32[]{:S(2)}) async-start(), calls=%async_computation.11 | async-start | bytes 4718592 | tf_op jit(solution)/shard_map/all_gather | solution.py:96
  447.6 43.7 %all-to-all-start.4 = ((bf16[8,192,256]{2,1,0:T(8,128)(2,1)}), bf16[8,192,256]{2,1,0:T(8,128)(2,1)S(1)}, u32[]{:S(2)}, u32[]{:S(2)}) async-start(bf16[8,192,256]{2,1,0:T(8,128)(2,1)} %all_to_all.116), calls=%async_computation.4 | async-start | bytes 1572864 | tf_op jit(solution)/shard_map/all_to_all | solution.py:84
  491.2 31.6 %all-to-all-start.5 = ((bf16[8,192,256]{2,1,0:T(8,128)(2,1)}), bf16[8,192,256]{2,1,0:T(8,128)(2,1)}, u32[]{:S(2)}, u32[]{:S(2)}) async-start(bf16[8,192,256]{2,1,0:T(8,128)(2,1)} %all_to_all.120), calls=%async_computation.5 | async-start | bytes 1572864 | tf_op jit(solution)/shard_map/all_to_all | solution.py:85
  522.8 24.4 %all-to-all-start.6 = ((bf16[8,192,256]{2,1,0:T(8,128)(2,1)}), bf16[8,192,256]{2,1,0:T(8,128)(2,1)S(1)}, u32[]{:S(2)}, u32[]{:S(2)}) async-start(bf16[8,192,256]{2,1,0:T(8,128)(2,1)} %all_to_all.124), calls=%async_computation.6 | async-start | bytes 1572864 | tf_op jit(solution)/shard_map/all_to_all | solution.py:86
Sparse Core Ops, SparseCore 0:
  9.8 90.1 all-gather.2
  261.6 184.5 reduce-scatter.1
  447.8 72.7 all-gather.4
where the time goes:
time: 561 us; the launch traced here: 559 us
  waiting for transfers between devices  332 us (59%)
  blocking collectives  58.8 us (10%)
  local copies, waits for them, and re-layouts  56.5 us (10%)
  matrix products  48.5 us (9%)
  starting transfers between devices  29.8 us (5%)
  other arithmetic  19.2 us (3%)
  between operations  14.6 us (3%)
    reduce_scatter x1, waiting for transfers between devices, local(): lax.psum_scatter(lax.dot_general(attn_out, out_grad, (((0,), (0,)), ((),...  185 us
    unnamed x1, blocking collectives  35.4 us
    all_gather x1, waiting for transfers between devices, local(): lax.all_gather(out_weight, 'dp', axis=0, tiled=True)  34.7 us
    all_to_all x1, waiting for transfers between devices, local(): lax.all_to_all(query_grad_h, 'seq', split_axis=0, concat_axis=1, tiled=True)  31.4 us
    all_to_all x1, blocking collectives, local(): lax.all_to_all(out_head, 'seq', split_axis=0, concat_axis=1, tiled=True)  23.4 us
    all_to_all x1, waiting for transfers between devices, local(): lax.all_to_all(key_grad_h, 'seq', split_axis=0, concat_axis=1, tiled=True)  22.5 us
    all_to_all x1, waiting for transfers between devices, local(): lax.all_to_all(queries, 'seq', split_axis=1, concat_axis=0, tiled=True)  20 us
    all_to_all x1, waiting for transfers between devices, local(): lax.all_to_all(keys, 'seq', split_axis=1, concat_axis=0, tiled=True)  19.9 us
  transfers between devices with their start and end apart: 10, of which 7 were waited for; matrix products, arithmetic and copies ran while one was open for 6% of the time, Pallas kernels for 0%

commit v1 on v0

--- a/solution.py
+++ b/solution.py
@@ -20,10 +20,14 @@
         lax.all_to_all(values, "seq", split_axis=1, concat_axis=0, tiled=True),
     )
     grad_h = lax.all_to_all(attn_grad, "seq", split_axis=1, concat_axis=0, tiled=True)
-    sec_all, flag_all = (
-        lax.all_gather(section_ids, "seq", axis=0, tiled=True),
-        lax.all_gather(masked, "seq", axis=0, tiled=True),
-    )
+    n_seq = lax.axis_size("seq")
+    code = section_ids * 2 + masked
+    code_all = lax.all_to_all(
+        jnp.broadcast_to(code[None], (n_seq,) + code.shape), "seq", 0, 0, tiled=True
+    ).reshape(-1)
+    sec_all = code_all // 2
+    flag_all = code_all - 2 * sec_all
+    grad_plane = lax.all_gather(out_grad, "dp", axis=0, tiled=True)
     seq_span = query_h.shape[0]
     width_here = query_h.shape[1]
     heads_here = width_here // HEAD_DIM
@@ -85,15 +89,13 @@
         lax.all_to_all(key_grad_h, "seq", split_axis=0, concat_axis=1, tiled=True),
         lax.all_to_all(value_grad_h, "seq", split_axis=0, concat_axis=1, tiled=True),
     )
-    grad_share = lax.psum_scatter(
+    out_plane = lax.all_to_all(attn_out, "dp", split_axis=1, concat_axis=0, tiled=True)
+    weight_grad = lax.psum(
         lax.dot_general(
-            attn_out, out_grad, (((0,), (0,)), ((), ())), preferred_element_type=jnp.float32
+            out_plane, grad_plane, (((0,), (0,)), ((), ())), preferred_element_type=jnp.float32
         ),
-        ("dp", "seq"),
-        scatter_dimension=0,
-        tiled=True,
+        "seq",
     )
-    weight_grad = lax.all_gather(grad_share, "seq", axis=0, tiled=True)
     return (query_grad, key_grad, value_grad, weight_grad)
 
 

time: 561 us -> 407 us (0.73)
  waiting for transfers between devices: 332 us -> 243 us
  blocking collectives: 58.8 us -> 0 us
  local copies, waits for them, and re-layouts: 56.5 us -> 35.5 us
  starting transfers between devices: 29.8 us -> 39.8 us
  matrix products: 48.5 us -> 57.8 us
    reduce_scatter x1 -> x0, waiting for transfers between devices: 185 us -> none  [local(): lax.psum_scatter(lax.dot_general(attn_out, out_grad, (((0,), (0,)), ((),...]
    psum x0 -> x1, waiting for transfers between devices: none -> 65.3 us  [local(): lax.psum(lax.dot_general(out_plane, grad_plane, (((0,), (0,)), ((), ())),...]
    unnamed x1 -> x0, blocking collectives: 35.4 us -> none
    all_to_all x0 -> x3, waiting for transfers between devices: none -> 29.3 us  [the longest x1 18.5 us: local(): lax.all_to_all(out_head, 'seq', split_axis=0, concat_axis=1, tiled=True)]
    all_to_all x1 -> x0, blocking collectives: 23.4 us -> none  [local(): lax.all_to_all(out_head, 'seq', split_axis=0, concat_axis=1, tiled=True)]
    all_to_all x1, waiting for transfers between devices: 20 us -> 0.01 us  [local(): lax.all_to_all(queries, 'seq', split_axis=1, concat_axis=0, tiled=True)]
    all_to_all x1, waiting for transfers between devices: 0.01 us -> 19.9 us  [local(): lax.all_to_all(values, 'seq', split_axis=1, concat_axis=0, tiled=True)]
    all_to_all x1, waiting for transfers between devices: 0.01 us -> 17.5 us  [local(): lax.all_to_all(attn_grad, 'seq', split_axis=1, concat_axis=0, tiled=True)]
  transfers between devices with their start and end apart: 10 -> 13, of which waited for: 7 -> 11; matrix products, arithmetic and copies ran while one was open for 6% -> 23% of each run, Pallas kernels for 0% -> 0%
where the time goes in v1:
time: 407 us; the launch traced here: 406 us
  waiting for transfers between devices  243 us (60%)
  matrix products  57.8 us (14%)
  starting transfers between devices  39.8 us (10%)
  local copies, waits for them, and re-layouts  35.5 us (9%)
  other arithmetic  15.4 us (4%)
  between operations  14 us (3%)
    psum x1, waiting for transfers between devices, local(): lax.psum(lax.dot_general(out_plane, grad_plane, (((0,), (0,)), ((), ())),...  65.3 us
    all_to_all x1, waiting for transfers between devices, local(): lax.all_to_all(query_grad_h, 'seq', split_axis=0, concat_axis=1, tiled=True)  27.8 us
    all_gather x1, waiting for transfers between devices, local(): lax.all_gather(out_weight, 'dp', axis=0, tiled=True)  26.4 us
    all_to_all x1, waiting for transfers between devices, local(): lax.all_to_all(values, 'seq', split_axis=1, concat_axis=0, tiled=True)  19.9 us
    all_to_all x1, waiting for transfers between devices, local(): lax.all_to_all(keys, 'seq', split_axis=1, concat_axis=0, tiled=True)  19.9 us
    all_to_all x1, waiting for transfers between devices, local(): lax.all_to_all(key_grad_h, 'seq', split_axis=0, concat_axis=1, tiled=True)  18.9 us
    all_to_all x1, waiting for transfers between devices, local(): lax.all_to_all(out_head, 'seq', split_axis=0, concat_axis=1, tiled=True)  18.5 us
    all_to_all x1, waiting for transfers between devices, local(): lax.all_to_all(attn_grad, 'seq', split_axis=1, concat_axis=0, tiled=True)  17.5 us
  transfers between devices with their start and end apart: 13, of which 11 were waited for; matrix products, arithmetic and copies ran while one was open for 23% of the time, Pallas kernels for 0%

profile of v1, /device:TPU:0, one launch (start us, length us, event | category | flops | bytes accessed | tf_op | source)
XLA Modules:
  0.0 405.7 jit_solution(10119106563263983084)
XLA Ops:
  9.2 6.4 %all-to-all-start.1 = ((s32[8,1,192]{2,1,0:T(1,128)}), s32[8,1,192]{2,1,0:T(1,128)S(1)}, u32[]{:S(2)}, u32[]{:S(2)}) async-start(s32[8,1,192]{2,1,0:T(1,128)} %broadcast_in_dim.36), calls=%async_computation.1 | async-start | bytes 16384 | tf_op jit(solution)/shard_map/all_to_all | solution.py:25
  15.6 2.1 copy.117
  17.7 3.5 all-to-all-done.1
  21.2 3.6 all-to-all-start.2
  25.7 19.9 %all-to-all-done.2 = bf16[192,8,256]{2,0,1:T(8,128)(2,1)S(1)} async-done(((bf16[192,8,256]{2,0,1:T(8,128)(2,1)}), bf16[192,8,256]{2,0,1:T(8,128)(2,1)S(1)}, u32[]{:S(2)}, u32[]{:S(2)}) %all-to-all-start.2) | async-done | bytes 786464 | tf_op jit(solution)/shard_map/all_to_all | solution.py:19
  45.6 3.5 all-to-all-start.4
  50.1 19.9 %all-to-all-done.4 = bf16[192,8,256]{2,0,1:T(8,128)(2,1)S(1)} async-done(((bf16[192,8,256]{2,0,1:T(8,128)(2,1)}), bf16[192,8,256]{2,0,1:T(8,128)(2,1)S(1)}, u32[]{:S(2)}, u32[]{:S(2)}) %all-to-all-start.4) | async-done | bytes 786464 | tf_op jit(solution)/shard_map/all_to_all | solution.py:20
  70.1 3.5 all-to-all-start
  73.6 26.4 %all-gather.3.cloned.1.call-done = bf16[2048,2048]{1,0:T(8,128)(2,1)} async-done(((bf16[512,2048]{1,0:T(8,128)(2,1)}), bf16[2048,2048]{1,0:T(8,128)(2,1)}) %all-gather.3.cloned.1.call-update) | async-done | bytes 8388624 | tf_op jit(solution)/shard_map/all_gather | solution.py:13
  100.1 6.5 %convolution_convert_fusion.1 = bf16[192,2048]{1,0:T(8,128)(2,1)S(1)} fusion(bf16[192,2048]{1,0:T(8,128)(2,1)} %param.12, bf16[2048,2048]{1,0:T(8,128)(2,1)} %all-gather.3.cloned.1.call-done), kind=kOutput, calls=%fused_computation.31 | convolution fusion | flops 1611005952 | bytes 9961472 | tf_op jit(solution)/shard_map/dot_general | solution.py:11
  107.6 4.6 %all-to-all-start.3 = ((bf16[192,8,256]{2,0,1:T(8,128)(2,1)}), bf16[192,8,256]{2,0,1:T(8,128)(2,1)}, u32[]{:S(2)}, u32[]{:S(2)}) async-start(bf16[192,8,256]{2,0,1:T(8,128)(2,1)} %bitcast.76), calls=%async_computation.3 | async-start | bytes 1572864 | tf_op jit(solution)/shard_map/all_to_all | solution.py:22
  113.7 1.8 copy.68
  115.7 17.5 %all-to-all-done.3 = bf16[192,8,256]{2,0,1:T(8,128)(2,1)} async-done(((bf16[192,8,256]{2,0,1:T(8,128)(2,1)}), bf16[192,8,256]{2,0,1:T(8,128)(2,1)}, u32[]{:S(2)}, u32[]{:S(2)}) %all-to-all-start.3) | async-done | bytes 786464 | tf_op jit(solution)/shard_map/all_to_all | solution.py:22
  133.2 2.0 reshape.128
  135.2 65.2 %while.17 = (s32[]{:T(128)}, f32[1536,2,128]{0,2,1:T(8,128)}, f32[1536,2,128]{0,2,1:T(8,128)}, bf16[3,512,2,128]{3,2,1,0:T(2,128)(2,1)}, bf16[3,512,2,128]{3,2,1...) while((s32[]{:T(128)}, f32[1536,2,128]{0,2,1:T(8,128)}, ...), condition=%wide.region_4.5_spmd.clone, body=%wide.region_0.4_spmd.clone.sunk | while | flops 2435711488 | bytes 120883744 | solution.py:79
  136.1 5.0 %fusion.54 = (f32[2,512]{1,0:T(2,128)S(1)}, f32[2,512,1536]{2,1,0:T(8,128)}) fusion(pred[512,1536]{1,0:T(8,128)(4,1)S(1)} %compare_or_fusion.2, bf16[1536,2,128]{2,0,1:T(8,128)(2,1)S(1)} %get-tuple-element.300, bf16[1,512,2,128]{3,2,1,0:T(2,128)(2,1)S(1)} %constant_dynamic-slice_fusion.8), kind=kOutput, calls=%fused_computation.53.clone.1 | convolution fusion | flops 408946176 | bytes 8130560 | tf_op jit(solution)/shard_map/while/body/eval_jaxpr/sub | solution.py:50
  141.1 3.8 fusion.55
  147.5 2.1 fusion.58
  150.9 1.8 fusion.56
  153.4 1.9 fusion.57
  156.2 5.0 %fusion.54 = (f32[2,512]{1,0:T(2,128)S(1)}, f32[2,512,1536]{2,1,0:T(8,128)}) fusion(pred[512,1536]{1,0:T(8,128)(4,1)S(1)} %compare_or_fusion.2, bf16[1536,2,128]{2,0,1:T(8,128)(2,1)S(1)} %get-tuple-element.300, bf16[1,512,2,128]{3,2,1,0:T(2,128)(2,1)S(1)} %constant_dynamic-slice_fusion.8), kind=kOutput, calls=%fused_computation.53.clone.1 | convolution fusion | flops 408946176 | bytes 8130560 | tf_op jit(solution)/shard_map/while/body/eval_jaxpr/sub | solution.py:50
  161.2 3.8 fusion.55
  167.6 2.1 fusion.58
  171.0 3.3 fusion.56
  174.4 3.5 fusion.57
  178.7 5.0 %fusion.54 = (f32[2,512]{1,0:T(2,128)S(1)}, f32[2,512,1536]{2,1,0:T(8,128)}) fusion(pred[512,1536]{1,0:T(8,128)(4,1)S(1)} %compare_or_fusion.2, bf16[1536,2,128]{2,0,1:T(8,128)(2,1)S(1)} %get-tuple-element.300, bf16[1,512,2,128]{3,2,1,0:T(2,128)(2,1)S(1)} %constant_dynamic-slice_fusion.8), kind=kOutput, calls=%fused_computation.53.clone.1 | convolution fusion | flops 408946176 | bytes 8130560 | tf_op jit(solution)/shard_map/while/body/eval_jaxpr/sub | solution.py:50
  183.7 3.8 fusion.55
  190.1 2.1 fusion.58
  193.6 3.3 fusion.56
  196.9 3.5 fusion.57
  200.4 3.3 all_to_all.145
  203.7 3.8 all-to-all-start.8
  208.2 1.4 all_to_all.137
  209.6 18.5 %all-to-all-done.8 = bf16[8,192,256]{2,1,0:T(8,128)(2,1)S(1)} async-done(((bf16[8,192,256]{2,1,0:T(8,128)(2,1)}), bf16[8,192,256]{2,1,0:T(8,128)(2,1)S(1)}, u32[]{:S(2)}, u32[]{:S(2)}) %all-to-all-start.8) | async-done | bytes 786464 | tf_op jit(solution)/shard_map/all_to_all | solution.py:87
  228.1 3.5 all-to-all-start.6
  233.6 18.9 %all-to-all-done.6 = bf16[8,192,256]{2,1,0:T(8,128)(2,1)S(1)} async-done(((bf16[8,192,256]{2,1,0:T(8,128)(2,1)}), bf16[8,192,256]{2,1,0:T(8,128)(2,1)S(1)}, u32[]{:S(2)}, u32[]{:S(2)}) %all-to-all-start.6) | async-done | bytes 786464 | tf_op jit(solution)/shard_map/all_to_all | solution.py:89
  252.5 3.5 all-to-all-start.9
  256.0 1.5 convert_element_type.35
  258.1 1.4 all_to_all.141
  259.5 7.3 %all-to-all-done.9 = bf16[192,4,512]{2,0,1:T(8,128)(2,1)S(1)} async-done(((bf16[192,4,512]{2,0,1:T(8,128)(2,1)}), bf16[192,4,512]{2,0,1:T(8,128)(2,1)S(1)}, u32[]{:S(2)}, u32[]{:S(2)}) %all-to-all-start.9) | async-done | bytes 786464 | tf_op jit(solution)/shard_map/all_to_all | solution.py:92
  266.8 3.5 all-to-all-start.7
  270.5 5.7 %fusion.20 = f32[512,2048]{1,0:T(8,128)} fusion(bf16[768,512]{1,0:T(8,128)(2,1)S(1)} %bitcast.122, bf16[768,2048]{1,0:T(8,128)(2,1)} %all-gather.5.cloned.1.call-done), kind=kOutput, calls=%fused_computation.54 | convolution fusion | flops 1610612736 | bytes 8126464 | tf_op jit(solution)/shard_map/dot_general | solution.py:94
  277.3 1.4 all_to_all.133
  278.7 16.3 %all-to-all-done.7 = bf16[8,192,256]{2,1,0:T(8,128)(2,1)S(1)} async-done(((bf16[8,192,256]{2,1,0:T(8,128)(2,1)}), bf16[8,192,256]{2,1,0:T(8,128)(2,1)S(1)}, u32[]{:S(2)}, u32[]{:S(2)}) %all-to-all-start.7) | async-done | bytes 786464 | tf_op jit(solution)/shard_map/all_to_all | solution.py:90
  295.0 3.5 all-to-all-start.5
  300.5 27.8 %all-to-all-done.5 = bf16[8,192,256]{2,1,0:T(8,128)(2,1)S(1)} async-done(((bf16[8,192,256]{2,1,0:T(8,128)(2,1)}), bf16[8,192,256]{2,1,0:T(8,128)(2,1)S(1)}, u32[]{:S(2)}, u32[]{:S(2)}) %all-to-all-start.5) | async-done | bytes 786464 | tf_op jit(solution)/shard_map/all_to_all | solution.py:88
  329.2 65.3 %all-reduce.2.cloned.1.call-done = f32[512,2048]{1,0:T(8,128)} async-done(((f32[512,2048]{1,0:T(8,128)}), f32[512,2048]{1,0:T(8,128)}) %all-reduce.2.cloned.1.call-update) | async-done | bytes 4194320 | tf_op jit(solution)/shard_map/psum | solution.py:93
  394.5 4.7 %copy.149 = f32[512,2048]{1,0:T(8,128)} copy(f32[512,2048]{1,0:T(8,128)} %all-reduce.2.cloned.1.call-done) | data formatting | bytes 8388608
  (146 shorter events, 28.6 us)
Async XLA Ops:
  7.2 17.6 %copy-start.11 = (bf16[192,2048]{1,0:T(8,128)(2,1)S(1)}, bf16[192,2048]{1,0:T(8,128)(2,1)}, u32[]{:S(2)}) copy-start(bf16[192,2048]{1,0:T(8,128)(2,1)} %param.11) | copy-start | bytes 2359300
  7.2 92.9 %all-gather.3.cloned.1.call-start = ((), (), s32[]{:S(2)}) async-start(), calls=%async_computation.10 | async-start | bytes 10485760 | tf_op jit(solution)/shard_map/all_gather | solution.py:13
  9.2 12.0 %all-to-all-start.1 = ((s32[8,1,192]{2,1,0:T(1,128)}), s32[8,1,192]{2,1,0:T(1,128)S(1)}, u32[]{:S(2)}, u32[]{:S(2)}) async-start(s32[8,1,192]{2,1,0:T(1,128)} %broadcast_in_dim.36), calls=%async_computation.1 | async-start | bytes 16384 | tf_op jit(solution)/shard_map/all_to_all | solution.py:25
  15.6 33.6 %copy-start.12 = (bf16[192,2048]{1,0:T(8,128)(2,1)S(1)}, bf16[192,2048]{1,0:T(8,128)(2,1)}, u32[]{:S(2)}) copy-start(bf16[192,2048]{1,0:T(8,128)(2,1)} %param.9) | copy-start | bytes 2359300
  21.2 24.5 %all-to-all-start.2 = ((bf16[192,8,256]{2,0,1:T(8,128)(2,1)}), bf16[192,8,256]{2,0,1:T(8,128)(2,1)S(1)}, u32[]{:S(2)}, u32[]{:S(2)}) async-start(bf16[192,8,256]{2,0,1:T(8,128)(2,1)} %bitcast.77), calls=%async_computation.2 | async-start | bytes 1572864 | tf_op jit(solution)/shard_map/all_to_all | solution.py:19
  45.6 24.4 %all-to-all-start.4 = ((bf16[192,8,256]{2,0,1:T(8,128)(2,1)}), bf16[192,8,256]{2,0,1:T(8,128)(2,1)S(1)}, u32[]{:S(2)}, u32[]{:S(2)}) async-start(bf16[192,8,256]{2,0,1:T(8,128)(2,1)} %bitcast.75), calls=%async_computation.4 | async-start | bytes 1572864 | tf_op jit(solution)/shard_map/all_to_all | solution.py:20
  70.1 37.5 %all-to-all-start = ((bf16[192,8,256]{2,0,1:T(8,128)(2,1)}), bf16[192,8,256]{2,0,1:T(8,128)(2,1)S(1)}, u32[]{:S(2)}, u32[]{:S(2)}) async-start(bf16[192,8,256]{2,0,1:T(8,128)(2,1)} %bitcast.78), calls=%async_computation | async-start | bytes 1572864 | tf_op jit(solution)/shard_map/all_to_all | solution.py:18
  107.6 25.7 %all-to-all-start.3 = ((bf16[192,8,256]{2,0,1:T(8,128)(2,1)}), bf16[192,8,256]{2,0,1:T(8,128)(2,1)}, u32[]{:S(2)}, u32[]{:S(2)}) async-start(bf16[192,8,256]{2,0,1:T(8,128)(2,1)} %bitcast.76), calls=%async_computation.3 | async-start | bytes 1572864 | tf_op jit(solution)/shard_map/all_to_all | solution.py:22
  112.2 158.3 %all-gather.5.cloned.1.call-start = ((), (), s32[]{:S(2)}) async-start(), calls=%async_computation.11 | async-start | bytes 3932160 | tf_op jit(solution)/shard_map/all_gather | solution.py:30
  135.2 5.8 %copy-start.3 = (bf16[1536,2,128]{2,0,1:T(8,128)(2,1)}, bf16[1536,2,128]{2,0,1:T(8,128)(2,1)S(1)}, u32[]{:S(2)}) copy-start(bf16[1536,2,128]{2,0,1:T(8,128)(2,1)S(1)} %get-tuple-element.300) | copy-start | bytes 2359300 | tf_op jit(solution)/shard_map/while
  135.3 5.8 %copy-start.7 = (bf16[3,512,2,128]{3,2,1,0:T(2,128)(2,1)}, bf16[3,512,2,128]{3,2,1,0:T(2,128)(2,1)S(1)}, u32[]{:S(2)}) copy-start(bf16[3,512,2,128]{3,2,1,0:T(2,128)(2,1)S(1)} %get-tuple-element.296) | copy-start | bytes 2359300 | tf_op jit(solution)/shard_map/while
  135.3 9.6 %copy-start.9 = (bf16[3,512,2,128]{3,2,1,0:T(2,128)(2,1)}, bf16[3,512,2,128]{3,2,1,0:T(2,128)(2,1)S(1)}, u32[]{:S(2)}) copy-start(bf16[3,512,2,128]{3,2,1,0:T(2,128)(2,1)S(1)} %get-tuple-element.301) | copy-start | bytes 2359300 | tf_op jit(solution)/shard_map/while
  141.1 5.1 %slice-start = ((s8[6291456]{0:T(1024)(128)(4,1)}), s8[4194304]{0:T(1024)(128)(4,1)S(1)}, s32[]{:S(2)}) async-start(s8[6291456]{0:T(1024)(128)(4,1)} %bitcast.119), calls=%async_computation.13 | async-start | bytes 8388608 | tf_op jit(solution)/shard_map/while
  141.1 4.0 copy-start.13
  141.1 5.1 %slice-start.1 = ((s8[6291456]{0:T(1024)(128)(4,1)}), s8[2097152]{0:T(1024)(128)(4,1)S(1)}, s32[]{:S(2)}) async-start(s8[6291456]{0:T(1024)(128)(4,1)} %bitcast.119), calls=%async_computation.14 | async-start | bytes 4194304 | tf_op jit(solution)/shard_map/while
  144.9 2.6 copy-start
  150.9 2.5 copy-start.6
  155.3 5.8 %copy-start.3 = (bf16[1536,2,128]{2,0,1:T(8,128)(2,1)}, bf16[1536,2,128]{2,0,1:T(8,128)(2,1)S(1)}, u32[]{:S(2)}) copy-start(bf16[1536,2,128]{2,0,1:T(8,128)(2,1)S(1)} %get-tuple-element.300) | copy-start | bytes 2359300 | tf_op jit(solution)/shard_map/while
  155.3 5.8 %copy-start.7 = (bf16[3,512,2,128]{3,2,1,0:T(2,128)(2,1)}, bf16[3,512,2,128]{3,2,1,0:T(2,128)(2,1)S(1)}, u32[]{:S(2)}) copy-start(bf16[3,512,2,128]{3,2,1,0:T(2,128)(2,1)S(1)} %get-tuple-element.296) | copy-start | bytes 2359300 | tf_op jit(solution)/shard_map/while
  155.3 9.6 %copy-start.9 = (bf16[3,512,2,128]{3,2,1,0:T(2,128)(2,1)}, bf16[3,512,2,128]{3,2,1,0:T(2,128)(2,1)S(1)}, u32[]{:S(2)}) copy-start(bf16[3,512,2,128]{3,2,1,0:T(2,128)(2,1)S(1)} %get-tuple-element.301) | copy-start | bytes 2359300 | tf_op jit(solution)/shard_map/while
  161.2 5.1 %slice-start = ((s8[6291456]{0:T(1024)(128)(4,1)}), s8[4194304]{0:T(1024)(128)(4,1)S(1)}, s32[]{:S(2)}) async-start(s8[6291456]{0:T(1024)(128)(4,1)} %bitcast.119), calls=%async_computation.13 | async-start | bytes 8388608 | tf_op jit(solution)/shard_map/while
  161.2 4.0 copy-start.13
  161.2 5.1 %slice-start.1 = ((s8[6291456]{0:T(1024)(128)(4,1)}), s8[2097152]{0:T(1024)(128)(4,1)S(1)}, s32[]{:S(2)}) async-start(s8[6291456]{0:T(1024)(128)(4,1)} %bitcast.119), calls=%async_computation.14 | async-start | bytes 4194304 | tf_op jit(solution)/shard_map/while
  165.0 2.6 copy-start
  171.0 3.4 copy-start.1
  171.0 3.4 copy-start.6
  174.4 3.5 copy-start.4
  174.4 3.5 copy-start.8
  174.4 3.5 copy-start.10
  177.9 5.8 %copy-start.3 = (bf16[1536,2,128]{2,0,1:T(8,128)(2,1)}, bf16[1536,2,128]{2,0,1:T(8,128)(2,1)S(1)}, u32[]{:S(2)}) copy-start(bf16[1536,2,128]{2,0,1:T(8,128)(2,1)S(1)} %get-tuple-element.300) | copy-start | bytes 2359300 | tf_op jit(solution)/shard_map/while
  177.9 5.8 %copy-start.7 = (bf16[3,512,2,128]{3,2,1,0:T(2,128)(2,1)}, bf16[3,512,2,128]{3,2,1,0:T(2,128)(2,1)S(1)}, u32[]{:S(2)}) copy-start(bf16[3,512,2,128]{3,2,1,0:T(2,128)(2,1)S(1)} %get-tuple-element.296) | copy-start | bytes 2359300 | tf_op jit(solution)/shard_map/while
  177.9 9.6 %copy-start.9 = (bf16[3,512,2,128]{3,2,1,0:T(2,128)(2,1)}, bf16[3,512,2,128]{3,2,1,0:T(2,128)(2,1)S(1)}, u32[]{:S(2)}) copy-start(bf16[3,512,2,128]{3,2,1,0:T(2,128)(2,1)S(1)} %get-tuple-element.301) | copy-start | bytes 2359300 | tf_op jit(solution)/shard_map/while
  183.7 5.1 %slice-start = ((s8[6291456]{0:T(1024)(128)(4,1)}), s8[4194304]{0:T(1024)(128)(4,1)S(1)}, s32[]{:S(2)}) async-start(s8[6291456]{0:T(1024)(128)(4,1)} %bitcast.119), calls=%async_computation.13 | async-start | bytes 8388608 | tf_op jit(solution)/shard_map/while
  183.7 4.0 copy-start.13
  183.7 5.1 %slice-start.1 = ((s8[6291456]{0:T(1024)(128)(4,1)}), s8[2097152]{0:T(1024)(128)(4,1)S(1)}, s32[]{:S(2)}) async-start(s8[6291456]{0:T(1024)(128)(4,1)} %bitcast.119), calls=%async_computation.14 | async-start | bytes 4194304 | tf_op jit(solution)/shard_map/while
  187.5 2.6 copy-start
  193.6 3.3 copy-start.1
  193.6 3.3 copy-start.6
  196.9 3.5 copy-start.4
  196.9 3.5 copy-start.8
  196.9 3.5 copy-start.10
  200.4 7.0 %copy-start.2 = (f32[1536,2,128]{0,2,1:T(8,128)S(1)}, f32[1536,2,128]{0,2,1:T(8,128)}, u32[]{:S(2)}) copy-start(f32[1536,2,128]{0,2,1:T(8,128)} %get-tuple-element.70) | copy-start | bytes 4718596
  203.7 24.4 %all-to-all-start.8 = ((bf16[8,192,256]{2,1,0:T(8,128)(2,1)}), bf16[8,192,256]{2,1,0:T(8,128)(2,1)S(1)}, u32[]{:S(2)}, u32[]{:S(2)}) async-start(bf16[8,192,256]{2,1,0:T(8,128)(2,1)} %all_to_all.145), calls=%async_computation.8 | async-start | bytes 1572864 | tf_op jit(solution)/shard_map/all_to_all | solution.py:87
  228.1 24.4 %all-to-all-start.6 = ((bf16[8,192,256]{2,1,0:T(8,128)(2,1)}), bf16[8,192,256]{2,1,0:T(8,128)(2,1)S(1)}, u32[]{:S(2)}, u32[]{:S(2)}) async-start(bf16[8,192,256]{2,1,0:T(8,128)(2,1)} %all_to_all.137), calls=%async_computation.6 | async-start | bytes 1572864 | tf_op jit(solution)/shard_map/all_to_all | solution.py:89
  252.5 14.3 %all-to-all-start.9 = ((bf16[192,4,512]{2,0,1:T(8,128)(2,1)}), bf16[192,4,512]{2,0,1:T(8,128)(2,1)S(1)}, u32[]{:S(2)}, u32[]{:S(2)}) async-start(bf16[192,4,512]{2,0,1:T(8,128)(2,1)} %copy.77), calls=%async_computation.9 | async-start | bytes 1572864 | tf_op jit(solution)/shard_map/all_to_all | solution.py:92
  266.8 28.1 %all-to-all-start.7 = ((bf16[8,192,256]{2,1,0:T(8,128)(2,1)}), bf16[8,192,256]{2,1,0:T(8,128)(2,1)S(1)}, u32[]{:S(2)}, u32[]{:S(2)}) async-start(bf16[8,192,256]{2,1,0:T(8,128)(2,1)} %all_to_all.141), calls=%async_computation.7 | async-start | bytes 1572864 | tf_op jit(solution)/shard_map/all_to_all | solution.py:90
  270.4 124.1 %all-reduce.2.cloned.1.call-start = ((), (), s32[]{:S(2)}) async-start(), calls=%async_computation.12 | async-start | bytes 8388608 | tf_op jit(solution)/shard_map/psum | solution.py:93
  295.0 33.3 %all-to-all-start.5 = ((bf16[8,192,256]{2,1,0:T(8,128)(2,1)}), bf16[8,192,256]{2,1,0:T(8,128)(2,1)S(1)}, u32[]{:S(2)}, u32[]{:S(2)}) async-start(bf16[8,192,256]{2,1,0:T(8,128)(2,1)} %all_to_all.133), calls=%async_computation.5 | async-start | bytes 1572864 | tf_op jit(solution)/shard_map/all_to_all | solution.py:88
  (8 other events, 16.5 us)
Sparse Core Ops, SparseCore 0:
  9.8 90.1 all-gather.2
  114.8 44.3 all-gather.4
  276.3 118.0 all-reduce.1
